TPU v7x, 256 devices: a whole 4x4x8 slice. The times are simulated.
256 devices in a mesh: outer: 4 (over y_hi, core), dp: 4 (over x), mp: 16 (over z, y_lo).
Axes of the slice: x: 4, y: 4 (y_hi: 2, y_lo: 2; y = y_hi * 2 + y_lo), z: 8, core: 2. Of those that a mesh axis runs over, the one named last changes fastest.
Arguments:
- tokens: bfloat16 [4, 4096, 2048], P('outer', 'dp'), may hold values from -6 to 6
- cotangent: bfloat16 [4, 4096, 2048], P('outer', 'dp'), may hold values from -0.59765625 to 0.59765625
- gate_weight: bfloat16 [4, 2048, 6144], P('outer', 'dp', 'mp'), may hold values from -0.125 to 0.125
- up_weight: bfloat16 [4, 2048, 6144], P('outer', 'dp', 'mp'), may hold values from -0.125 to 0.125
- down_master: float32 [4, 6144, 2048], P('outer', 'mp', 'dp'), may hold values from -0.0375 to 0.0375
- first_moment: float32 [4, 6144, 2048], P('outer', 'mp', 'dp'), may hold values from -0.6 to 0.6
- second_moment: float32 [4, 6144, 2048], P('outer', 'mp', 'dp'), may hold values from 1 to 10
- anchor: float32 [6144, 2048], P('mp', 'dp'), may hold values from -0.0375 to 0.0375
- outer_momentum: float32 [6144, 2048], P('mp', 'dp'), may hold values from -0.00018 to 0.00018
Outputs:
- new_params: float32 [6144, 2048], P('mp', 'dp')
- first_out: float32 [4, 6144, 2048], P('outer', 'mp', 'dp')
- second_out: float32 [4, 6144, 2048], P('outer', 'mp', 'dp')
- momentum_out: float32 [6144, 2048], P('mp', 'dp')
- input_grad: bfloat16 [4, 4096, 2048], P('outer', ('dp', 'mp'))
All inputs are finite; a program needn't handle non-finite values.
Results may differ from a plain program's by a relative error of at most 0.023.
Values may be sent and summed in bfloat16 or wider, within the bound.
No kernel may reach another device: no remote copies, remote signals or barrier semaphores. Data moves between devices by JAX's collectives and lax.ppermute only.
A program may use at most 128 MiB of HBM per device.

v0:
```python
import jax
import jax.numpy as jnp
from jax import lax
from jax.sharding import PartitionSpec as P

bias_one = 1.0 - (0.9**50) ** 2
bias_two = 1.0 - (0.999**50) ** 2


def shards(
    tokens,
    cotangent,
    gate_weight,
    up_weight,
    down_master,
    first_moment,
    second_moment,
    anchor,
    outer_momentum,
):
    inputs = tokens[0]
    upstream = cotangent[0]
    gate_full, up_full = (
        lax.all_gather(gate_weight[0], "dp", axis=0, tiled=True),
        lax.all_gather(up_weight[0], "dp", axis=0, tiled=True),
    )
    gate_pre = jnp.dot(inputs, gate_full, preferred_element_type=jnp.float32)
    up_pre = jnp.dot(inputs, up_full, preferred_element_type=jnp.float32)
    gate_sigmoid = jax.nn.sigmoid(gate_pre)
    active = gate_pre * gate_sigmoid
    hidden = (active * up_pre).astype(jnp.bfloat16)
    master = down_master[0]
    down_half = master.astype(jnp.bfloat16)
    grad_hidden = lax.dot_general(
        upstream,
        lax.all_gather(down_half, "dp", axis=1, tiled=True),
        (((1,), (1,)), ((), ())),
        preferred_element_type=jnp.float32,
    )
    grad_up = (grad_hidden * active).astype(jnp.bfloat16)
    grad_gate = (
        grad_hidden * up_pre * gate_sigmoid * (1.0 + gate_pre * (1.0 - gate_sigmoid))
    ).astype(jnp.bfloat16)
    first_part = lax.dot_general(
        grad_gate, gate_full, (((1,), (1,)), ((), ())), preferred_element_type=jnp.float32
    )
    second_part = lax.dot_general(
        grad_up, up_full, (((1,), (1,)), ((), ())), preferred_element_type=jnp.float32
    )
    input_grad = lax.psum_scatter(
        (first_part + second_part).astype(jnp.bfloat16), "mp", scatter_dimension=0, tiled=True
    )
    full_grad = lax.dot_general(
        hidden, upstream, (((0,), (0,)), ((), ())), preferred_element_type=jnp.float32
    )
    grad_down = lax.psum_scatter(
        full_grad.astype(jnp.bfloat16), "dp", scatter_dimension=1, tiled=True
    ).astype(jnp.float32)
    first_new = 0.9 * first_moment[0] + 0.1 * grad_down
    second_new = 0.999 * second_moment[0] + 0.001 * grad_down * grad_down
    adam_step = first_new / bias_one / (jnp.sqrt(second_new / bias_two) + 1e-08) + 0.1 * master
    inner_params = master - 0.001 * adam_step
    drift_local = anchor - inner_params
    mean_drift = lax.psum(drift_local.astype(jnp.bfloat16), "outer").astype(
        jnp.float32
    ) / lax.axis_size("outer")
    momentum_out = 0.9 * outer_momentum + mean_drift
    new_params = anchor - 0.7 * (mean_drift + 0.9 * momentum_out)
    return (new_params, first_new[None], second_new[None], momentum_out, input_grad[None])


def solution(mesh):
    return jax.shard_map(
        shards,
        mesh=mesh,
        in_specs=(
            P("outer", "dp", None),
            P("outer", "dp", None),
            P("outer", "dp", "mp"),
            P("outer", "dp", "mp"),
            P("outer", "mp", "dp"),
            P("outer", "mp", "dp"),
            P("outer", "mp", "dp"),
            P("mp", "dp"),
            P("mp", "dp"),
        ),
        out_specs=(
            P("mp", "dp"),
            P("outer", "mp", "dp"),
            P("outer", "mp", "dp"),
            P("mp", "dp"),
            P("outer", ("dp", "mp"), None),
        ),
        check_vma=False,
    )
```

profile of v0, /device:TPU:2, one launch (start us, length us, event | category | flops | bytes accessed | tf_op | source)
XLA Modules:
  0.0 295.2 jit_solution(9334009142262254615)
XLA Ops:
  7.2 0.0 all-gather.8.cloned.1.call-start
  7.2 0.7 all-gather.8.cloned.1.call-update
  7.9 0.0 all-gather.10.cloned.1.call-start
  7.9 0.7 all-gather.10.cloned.1.call-update
  8.6 0.0 all-gather.6.cloned.1.call-start
  8.7 1.9 bitcast_convert_fusion
  10.6 0.0 all-gather.6.cloned.1.call-update
  10.6 0.0 reduce-scatter.3.cloned.1.call-start
  10.7 30.1 %all-gather.8.cloned.1.call-done = bf16[1,2048,384]{2,1,0:T(8,128)(2,1)} async-done(((bf16[1,512,384]{2,1,0:T(8,128)(2,1)}), bf16[1,2048,384]{2,1,0:T(8,128)(2,1)}) %all-gather.8.cloned.1.call-update) | async-done | bytes 1572880 | tf_op jit(solution)/shard_map/all_gather | solution.py:24
  40.8 5.0 %fusion.6 = f32[1024,384]{1,0:T(8,128)S(1)} fusion(bf16[1,1024,2048]{2,1,0:T(8,128)(2,1)} %param.9, bf16[1,2048,384]{2,1,0:T(8,128)(2,1)} %all-gather.8.cloned.1.call-done), kind=kOutput, calls=%fused_computation.7 | convolution fusion | flops 1610612736 | bytes 7340032 | tf_op jit(solution)/shard_map/dot_general | solution.py:27
  45.8 26.0 %all-gather.10.cloned.1.call-done = bf16[1,2048,384]{2,1,0:T(8,128)(2,1)} async-done(((bf16[1,512,384]{2,1,0:T(8,128)(2,1)}), bf16[1,2048,384]{2,1,0:T(8,128)(2,1)}) %all-gather.10.cloned.1.call-update) | async-done | bytes 1572880 | tf_op jit(solution)/shard_map/all_gather | solution.py:25
  71.8 0.0 copy-start.3
  71.8 5.1 %fusion.4 = f32[1024,384]{1,0:T(8,128)S(1)} fusion(bf16[1,1024,2048]{2,1,0:T(8,128)(2,1)} %param.9, bf16[1,2048,384]{2,1,0:T(8,128)(2,1)} %all-gather.10.cloned.1.call-done), kind=kOutput, calls=%fused_computation.5 | convolution fusion | flops 1610612736 | bytes 7340032 | tf_op jit(solution)/shard_map/dot_general | solution.py:28
  77.0 0.0 copy-start
  77.0 1.1 copy-done
  78.1 0.0 copy-done.3
  78.1 3.2 %fusion.8 = bf16[384,2048]{1,0:T(8,128)(2,1)} fusion(bf16[1,1024,2048]{2,1,0:T(8,128)(2,1)S(1)} %copy-done.3, f32[1024,384]{1,0:T(8,128)S(1)} %fusion.4, f32[1024,384]{1,0:T(8,128)S(1)} %fusion.6), kind=kOutput, calls=%fused_computation.9 | convolution fusion | flops 1613758464 | bytes 8912896 | tf_op jit(solution)/shard_map/dot_general | solution.py:53
  81.4 0.0 reduce-scatter.3.cloned.1.call-update
  81.4 0.0 all-reduce.2.cloned.1.call-start
  81.4 22.0 %all-gather.6.cloned.1.call-done = bf16[384,2048]{1,0:T(8,128)(2,1)} async-done(((bf16[384,512]{1,0:T(8,128)(2,1)}), bf16[384,2048]{1,0:T(8,128)(2,1)}) %all-gather.6.cloned.1.call-update) | async-done | bytes 1572880 | tf_op jit(solution)/shard_map/all_gather | solution.py:36
  103.4 5.0 %fusion = f32[1024,384]{1,0:T(8,128)S(1)} fusion(bf16[384,2048]{1,0:T(8,128)(2,1)} %all-gather.6.cloned.1.call-done, bf16[1,1024,2048]{2,1,0:T(8,128)(2,1)} %param.10), kind=kOutput, calls=%fused_computation.1 | convolution fusion | flops 1610612736 | bytes 7340032 | tf_op jit(solution)/shard_map/dot_general | solution.py:34
  108.4 7.9 %fusion.13 = f32[1024,2048]{1,0:T(8,128)} fusion(bf16[1,2048,384]{2,1,0:T(8,128)(2,1)} %all-gather.8.cloned.1.call-done, f32[1024,384]{1,0:T(8,128)S(1)} %fusion.6, f32[1024,384]{1,0:T(8,128)S(1)} %fusion, f32[1024,384]{1,0:T(8,128)} %copy-done), kind=kOutput, calls=%fused_computation.12 | convolution fusion | flops 1614544896 | bytes 14680064 | tf_op jit(solution)/shard_map/dot_general | solution.py:44
  116.3 17.5 %reduce-scatter.3.cloned.1.call-done = bf16[384,512]{1,0:T(8,128)(2,1)} async-done(((bf16[384,2048]{1,0:T(8,128)(2,1)}), bf16[384,512]{1,0:T(8,128)(2,1)}) %reduce-scatter.3.cloned.1.call-update) | async-done | bytes 393232 | tf_op jit(solution)/shard_map/reduce_scatter | solution.py:56
  133.8 3.9 %fusion.25 = (f32[1,384,512]{2,1,0:T(8,128)}, bf16[384,512]{1,0:T(8,128)(2,1)}, f32[1,384,512]{2,1,0:T(8,128)}) fusion(bf16[384,512]{1,0:T(8,128)(2,1)} %reduce-scatter.3.cloned.1.call-done, f32[1,384,512]{2,1,0:T(8,128)} %param.15, f32[384,512]{1,0:T(8,128)} %param.16, f32[1,384,512]{2,1,0:T(8,128)} %param.14, f32[1,384,512]{2,1,0:T(8,128)} %param.13), kind=kLoop, calls=%fused_computation.36 | loop fusion | flops 3538944 | bytes 5505024 | tf_op jit(solution)/shard_map/broadcast_in_dim | solution.py:69
  137.7 0.0 all-reduce.2.cloned.1.call-update
  137.8 0.0 reduce-scatter.5.cloned.1.call-start
  137.8 8.3 %add_convert_fusion = bf16[1024,2048]{1,0:T(8,128)(2,1)} fusion(f32[1024,2048]{1,0:T(8,128)} %fusion.13, bf16[1,2048,384]{2,1,0:T(8,128)(2,1)} %all-gather.10.cloned.1.call-done, f32[1024,384]{1,0:T(8,128)S(1)} %fusion, f32[1024,384]{1,0:T(8,128)S(1)} %fusion.6), kind=kOutput, calls=%fused_computation | convolution fusion | flops 1617166336 | bytes 17301504 | tf_op jit(solution)/shard_map/dot_general | solution.py:47
  146.1 0.0 copy-start.1
  146.1 0.0 copy-start.2
  146.1 0.0 reduce-scatter.5.cloned.1.call-update
  146.2 39.4 %all-reduce.2.cloned.1.call-done = bf16[384,512]{1,0:T(8,128)(2,1)} async-done(((bf16[384,512]{1,0:T(8,128)(2,1)}), bf16[384,512]{1,0:T(8,128)(2,1)}) %all-reduce.2.cloned.1.call-update) | async-done | bytes 393232 | tf_op jit(solution)/shard_map/psum | solution.py:64
  185.6 0.0 copy-done.1
  185.6 0.0 copy-done.2
  185.6 2.4 multiply_subtract_fusion
  188.0 100.4 %reduce-scatter.5.cloned.1.call-done = bf16[64,2048]{1,0:T(8,128)(2,1)} async-done(((bf16[1024,2048]{1,0:T(8,128)(2,1)}), bf16[64,2048]{1,0:T(8,128)(2,1)}) %reduce-scatter.5.cloned.1.call-update) | async-done | bytes 262160 | tf_op jit(solution)/shard_map/reduce_scatter | solution.py:50
Async XLA Ops:
  7.2 33.7 %all-gather.8.cloned.1.call-start = ((), (), s32[]{:S(2)}) async-start(), calls=%async_computation.6 | async-start | bytes 1966080 | tf_op jit(solution)/shard_map/all_gather | solution.py:24
  7.9 63.9 %all-gather.10.cloned.1.call-start = ((), (), s32[]{:S(2)}) async-start(), calls=%async_computation.7 | async-start | bytes 1966080 | tf_op jit(solution)/shard_map/all_gather | solution.py:25
  8.6 94.8 %all-gather.6.cloned.1.call-start = ((), (), s32[]{:S(2)}) async-start(), calls=%async_computation.4 | async-start | bytes 1966080 | tf_op jit(solution)/shard_map/all_gather | solution.py:36
  10.6 123.2 %reduce-scatter.3.cloned.1.call-start = ((), (), s32[]{:S(2)}) async-start(), calls=%async_computation.2 | async-start | bytes 1966080 | tf_op jit(solution)/shard_map/reduce_scatter | solution.py:56
  71.8 6.3 %copy-start.3 = (bf16[1,1024,2048]{2,1,0:T(8,128)(2,1)S(1)}, bf16[1,1024,2048]{2,1,0:T(8,128)(2,1)}, u32[]{:S(2)}) copy-start(bf16[1,1024,2048]{2,1,0:T(8,128)(2,1)} %param.10) | copy-start | bytes 12582916
  77.0 1.2 copy-start
  81.4 104.2 %all-reduce.2.cloned.1.call-start = ((), (), s32[]{:S(2)}) async-start(), calls=%async_computation.3 | async-start | bytes 786432 | tf_op jit(solution)/shard_map/psum | solution.py:64
  137.8 150.6 %reduce-scatter.5.cloned.1.call-start = ((), (), s32[]{:S(2)}) async-start(), calls=%async_computation.5 | async-start | bytes 4456448 | tf_op jit(solution)/shard_map/reduce_scatter | solution.py:50
  146.1 39.4 %copy-start.1 = (f32[384,512]{1,0:T(8,128)S(1)}, f32[384,512]{1,0:T(8,128)}, u32[]{:S(2)}) copy-start(f32[384,512]{1,0:T(8,128)} %param.16) | copy-start | bytes 2359300
  146.1 39.4 %copy-start.2 = (f32[384,512]{1,0:T(8,128)S(1)}, f32[384,512]{1,0:T(8,128)}, u32[]{:S(2)}) copy-start(f32[384,512]{1,0:T(8,128)} %param.17) | copy-start | bytes 2359300
Sparse Core Ops, SparseCore 0:
  9.8 30.9 all-gather.7
  42.6 29.1 all-gather.9
  74.2 29.1 all-gather.5
  105.8 27.9 reduce-scatter.2
  137.9 47.6 all-reduce.1
  188.7 99.5 reduce-scatter.4
where the time goes:
time: 295 us
  waiting for transfers between devices  237 us (80%)
  matrix products  34.6 us (12%)
  between operations  14.1 us (5%)
  other arithmetic  8.25 us (3%)
    reduce_scatter x1, waiting for transfers between devices, shards(): lax.psum_scatter((first_part + second_part).astype(jnp.bfloat16), 'mp', s...  100 us
    psum x1, waiting for transfers between devices, shards(): lax.psum(drift_local.astype(jnp.bfloat16), 'outer').astype(jnp.float32)  39.4 us
    all_gather x1, waiting for transfers between devices, shards(): lax.all_gather(gate_weight[0], 'dp', axis=0, tiled=True)  30.1 us
    all_gather x1, waiting for transfers between devices, shards(): lax.all_gather(up_weight[0], 'dp', axis=0, tiled=True)  26 us
    all_gather x1, waiting for transfers between devices, shards(): lax.all_gather(down_half, 'dp', axis=1, tiled=True)  22 us
    reduce_scatter x1, waiting for transfers between devices, shards(): lax.psum_scatter(full_grad.astype(jnp.bfloat16), 'dp', scatter_dimension=...  17.5 us
    dot_general x1, matrix products, shards(): lax.dot_general(grad_up, up_full, (((1,), (1,)), ((), ())), preferred_ele...  8.32 us
    dot_general x1, matrix products, shards(): lax.dot_general(grad_gate, gate_full, (((1,), (1,)), ((), ())), preferred...  7.85 us
  transfers between devices with their start and end apart: 6, of which 6 were waited for; matrix products, arithmetic and copies ran while one was open for 13% of the time, Pallas kernels for 0%

commit v1 on v0

--- a/solution.py
+++ b/solution.py
@@ -61,7 +61,7 @@
     adam_step = first_new / bias_one / (jnp.sqrt(second_new / bias_two) + 1e-08) + 0.1 * master
     inner_params = master - 0.001 * adam_step
     drift_local = anchor - inner_params
-    mean_drift = lax.psum(drift_local.astype(jnp.bfloat16), "outer").astype(
+    mean_drift = jnp.sum(lax.all_gather(drift_local.astype(jnp.bfloat16), "outer"), axis=0).astype(
         jnp.float32
     ) / lax.axis_size("outer")
     momentum_out = 0.9 * outer_momentum + mean_drift

time: 295 us -> 279 us (0.946)
  matrix products: 34.6 us -> 25.4 us
  waiting for transfers between devices: 237 us -> 230 us
    psum x1 -> x0, waiting for transfers between devices: 39.4 us -> none  [shards(): lax.psum(drift_local.astype(jnp.bfloat16), 'outer').astype(jnp.float32)]
    all_gather x0 -> x1, waiting for transfers between devices: none -> 17.5 us  [shards(): lax.all_gather(drift_local.astype(jnp.bfloat16), 'outer')]
    reduce_scatter x1, waiting for transfers between devices: 17.5 us -> 26.1 us  [shards(): lax.psum_scatter(full_grad.astype(jnp.bfloat16), 'dp', scatter_dimension=...]
    all_gather x1, waiting for transfers between devices: 22 us -> 27.4 us  [shards(): lax.all_gather(down_half, 'dp', axis=1, tiled=True)]
    dot_general x1, matrix products: 7.85 us -> 2.62 us  [shards(): lax.dot_general(grad_gate, gate_full, (((1,), (1,)), ((), ())), preferred...]
    dot_general x1, matrix products: 8.32 us -> 4.35 us  [shards(): lax.dot_general(grad_up, up_full, (((1,), (1,)), ((), ())), preferred_ele...]
  transfers between devices with their start and end apart: 6 -> 6, of which waited for: 6 -> 6; matrix products, arithmetic and copies ran while one was open for 13% -> 9% of each run, Pallas kernels for 0% -> 0%
where the time goes in v1:
time: 279 us
  waiting for transfers between devices  230 us (82%)
  matrix products  25.4 us (9%)
  between operations  14.2 us (5%)
  other arithmetic  9.07 us (3%)
    reduce_scatter x1, waiting for transfers between devices, shards(): lax.psum_scatter((first_part + second_part).astype(jnp.bfloat16), 'mp', s...  99.3 us
    all_gather x1, waiting for transfers between devices, shards(): lax.all_gather(gate_weight[0], 'dp', axis=0, tiled=True)  32.1 us
    all_gather x1, waiting for transfers between devices, shards(): lax.all_gather(down_half, 'dp', axis=1, tiled=True)  27.4 us
    reduce_scatter x1, waiting for transfers between devices, shards(): lax.psum_scatter(full_grad.astype(jnp.bfloat16), 'dp', scatter_dimension=...  26.1 us
    all_gather x1, waiting for transfers between devices, shards(): lax.all_gather(up_weight[0], 'dp', axis=0, tiled=True)  26 us
    all_gather x1, waiting for transfers between devices, shards(): lax.all_gather(drift_local.astype(jnp.bfloat16), 'outer')  17.5 us
  transfers between devices with their start and end apart: 6, of which 6 were waited for; matrix products, arithmetic and copies ran while one was open for 9% of the time, Pallas kernels for 0%

profile of v1, /device:TPU:2, one launch (start us, length us, event | category | flops | bytes accessed | tf_op | source)
XLA Modules:
  0.0 278.8 jit_solution(5992988175032605682)
XLA Ops:
  7.2 0.0 all-gather.10.cloned.1.call-start
  7.2 0.7 all-gather.10.cloned.1.call-update
  7.9 0.0 all-gather.12.cloned.1.call-start
  7.9 0.7 all-gather.12.cloned.1.call-update
  8.6 0.0 reduce-scatter.3.cloned.1.call-start
  8.7 32.1 %all-gather.10.cloned.1.call-done = bf16[1,2048,384]{2,1,0:T(8,128)(2,1)} async-done(((bf16[1,512,384]{2,1,0:T(8,128)(2,1)}), bf16[1,2048,384]{2,1,0:T(8,128)(2,1)}) %all-gather.10.cloned.1.call-update) | async-done | bytes 1572880 | tf_op jit(solution)/shard_map/all_gather | solution.py:24
  40.8 5.0 %fusion.6 = f32[1024,384]{1,0:T(8,128)S(1)} fusion(bf16[1,1024,2048]{2,1,0:T(8,128)(2,1)} %param.9, bf16[1,2048,384]{2,1,0:T(8,128)(2,1)} %all-gather.10.cloned.1.call-done), kind=kOutput, calls=%fused_computation.7 | convolution fusion | flops 1610612736 | bytes 7340032 | tf_op jit(solution)/shard_map/dot_general | solution.py:27
  45.8 26.0 %all-gather.12.cloned.1.call-done = bf16[1,2048,384]{2,1,0:T(8,128)(2,1)} async-done(((bf16[1,512,384]{2,1,0:T(8,128)(2,1)}), bf16[1,2048,384]{2,1,0:T(8,128)(2,1)}) %all-gather.12.cloned.1.call-update) | async-done | bytes 1572880 | tf_op jit(solution)/shard_map/all_gather | solution.py:25
  71.8 0.0 copy-start.4
  71.8 5.1 %fusion.4 = f32[1024,384]{1,0:T(8,128)S(1)} fusion(bf16[1,1024,2048]{2,1,0:T(8,128)(2,1)} %param.9, bf16[1,2048,384]{2,1,0:T(8,128)(2,1)} %all-gather.12.cloned.1.call-done), kind=kOutput, calls=%fused_computation.5 | convolution fusion | flops 1610612736 | bytes 7340032 | tf_op jit(solution)/shard_map/dot_general | solution.py:28
  77.0 0.0 copy-done.4
  77.0 3.2 %fusion.8 = bf16[384,2048]{1,0:T(8,128)(2,1)} fusion(bf16[1,1024,2048]{2,1,0:T(8,128)(2,1)S(1)} %copy-done.4, f32[1024,384]{1,0:T(8,128)S(1)} %fusion.4, f32[1024,384]{1,0:T(8,128)S(1)} %fusion.6), kind=kOutput, calls=%fused_computation.9 | convolution fusion | flops 1613758464 | bytes 8912896 | tf_op jit(solution)/shard_map/dot_general | solution.py:53
  80.1 0.0 reduce-scatter.3.cloned.1.call-update
  80.2 0.0 all-gather.8.cloned.1.call-start
  80.2 1.9 bitcast_convert_fusion
  82.1 0.0 all-gather.8.cloned.1.call-update
  82.2 0.0 all-gather.14.cloned.1.call-start
  82.2 26.1 %reduce-scatter.3.cloned.1.call-done = bf16[384,512]{1,0:T(8,128)(2,1)} async-done(((bf16[384,2048]{1,0:T(8,128)(2,1)}), bf16[384,512]{1,0:T(8,128)(2,1)}) %reduce-scatter.3.cloned.1.call-update) | async-done | bytes 393232 | tf_op jit(solution)/shard_map/reduce_scatter | solution.py:56
  108.3 3.9 %fusion.25 = (f32[1,384,512]{2,1,0:T(8,128)}, bf16[384,512]{1,0:T(8,128)(2,1)}, f32[1,384,512]{2,1,0:T(8,128)}) fusion(bf16[384,512]{1,0:T(8,128)(2,1)} %reduce-scatter.3.cloned.1.call-done, f32[1,384,512]{2,1,0:T(8,128)} %param.15, f32[384,512]{1,0:T(8,128)} %param.16, f32[1,384,512]{2,1,0:T(8,128)} %param.14, f32[1,384,512]{2,1,0:T(8,128)} %param.13), kind=kLoop, calls=%fused_computation.36 | loop fusion | flops 3538944 | bytes 5505024 | tf_op jit(solution)/shard_map/broadcast_in_dim | solution.py:69
  112.2 0.0 all-gather.14.cloned.1.call-update
  112.2 0.0 reduce-scatter.5.cloned.1.call-start
  112.3 27.4 %all-gather.8.cloned.1.call-done = bf16[384,2048]{1,0:T(8,128)(2,1)} async-done(((bf16[384,512]{1,0:T(8,128)(2,1)}), bf16[384,2048]{1,0:T(8,128)(2,1)}) %all-gather.8.cloned.1.call-update) | async-done | bytes 1572880 | tf_op jit(solution)/shard_map/all_gather | solution.py:36
  139.7 0.0 copy-start.2
  139.7 5.1 %fusion = f32[1024,384]{1,0:T(8,128)S(1)} fusion(bf16[384,2048]{1,0:T(8,128)(2,1)} %all-gather.8.cloned.1.call-done, bf16[1,1024,2048]{2,1,0:T(8,128)(2,1)} %param.10), kind=kOutput, calls=%fused_computation.1 | convolution fusion | flops 1610612736 | bytes 7340032 | tf_op jit(solution)/shard_map/dot_general | solution.py:34
  144.9 0.0 copy-done.2
  144.9 0.0 copy-start.1
  144.9 2.6 fusion.13
  147.5 0.0 copy-done.1
  147.5 4.4 %add_convert_fusion = bf16[1024,2048]{1,0:T(8,128)(2,1)} fusion(f32[1024,2048]{1,0:T(8,128)S(1)} %fusion.13, bf16[1,2048,384]{2,1,0:T(8,128)(2,1)S(1)} %copy-done.1, f32[1024,384]{1,0:T(8,128)S(1)} %fusion, f32[1024,384]{1,0:T(8,128)S(1)} %fusion.6), kind=kOutput, calls=%fused_computation | convolution fusion | flops 1617166336 | bytes 17301504 | tf_op jit(solution)/shard_map/dot_general | solution.py:47
  151.9 0.0 reduce-scatter.5.cloned.1.call-update
  151.9 0.0 copy-start
  151.9 0.0 copy-start.3
  151.9 17.5 %all-gather.14.cloned.1.call-done = bf16[1536,512]{1,0:T(8,128)(2,1)} async-done(((bf16[384,512]{1,0:T(8,128)(2,1)}), bf16[1536,512]{1,0:T(8,128)(2,1)}) %all-gather.14.cloned.1.call-update) | async-done | bytes 1572880 | tf_op jit(solution)/shard_map/all_gather | solution.py:64
  169.4 1.8 reduce_sum.12
  171.2 0.0 copy-done
  171.2 0.0 copy-done.3
  171.2 1.4 multiply_subtract_fusion
  172.7 99.3 %reduce-scatter.5.cloned.1.call-done = bf16[64,2048]{1,0:T(8,128)(2,1)} async-done(((bf16[1024,2048]{1,0:T(8,128)(2,1)}), bf16[64,2048]{1,0:T(8,128)(2,1)}) %reduce-scatter.5.cloned.1.call-update) | async-done | bytes 262160 | tf_op jit(solution)/shard_map/reduce_scatter | solution.py:50
Async XLA Ops:
  7.2 33.7 %all-gather.10.cloned.1.call-start = ((), (), s32[]{:S(2)}) async-start(), calls=%async_computation.5 | async-start | bytes 1966080 | tf_op jit(solution)/shard_map/all_gather | solution.py:24
  7.9 63.9 %all-gather.12.cloned.1.call-start = ((), (), s32[]{:S(2)}) async-start(), calls=%async_computation.6 | async-start | bytes 1966080 | tf_op jit(solution)/shard_map/all_gather | solution.py:25
  8.6 99.6 %reduce-scatter.3.cloned.1.call-start = ((), (), s32[]{:S(2)}) async-start(), calls=%async_computation.2 | async-start | bytes 1966080 | tf_op jit(solution)/shard_map/reduce_scatter | solution.py:56
  71.8 5.1 %copy-start.4 = (bf16[1,1024,2048]{2,1,0:T(8,128)(2,1)S(1)}, bf16[1,1024,2048]{2,1,0:T(8,128)(2,1)}, u32[]{:S(2)}) copy-start(bf16[1,1024,2048]{2,1,0:T(8,128)(2,1)} %param.10) | copy-start | bytes 12582916
  80.2 59.6 %all-gather.8.cloned.1.call-start = ((), (), s32[]{:S(2)}) async-start(), calls=%async_computation.3 | async-start | bytes 1966080 | tf_op jit(solution)/shard_map/all_gather | solution.py:36
  82.2 87.3 %all-gather.14.cloned.1.call-start = ((), (), s32[]{:S(2)}) async-start(), calls=%async_computation.7 | async-start | bytes 1966080 | tf_op jit(solution)/shard_map/all_gather | solution.py:64
  112.2 159.8 %reduce-scatter.5.cloned.1.call-start = ((), (), s32[]{:S(2)}) async-start(), calls=%async_computation.4 | async-start | bytes 4456448 | tf_op jit(solution)/shard_map/reduce_scatter | solution.py:50
  139.7 5.1 %copy-start.2 = (bf16[1,2048,384]{2,1,0:T(8,128)(2,1)S(1)}, bf16[1,2048,384]{2,1,0:T(8,128)(2,1)}, u32[]{:S(2)}) copy-start(bf16[1,2048,384]{2,1,0:T(8,128)(2,1)} %all-gather.10.cloned.1.call-done) | copy-start | bytes 4718596
  144.9 2.6 copy-start.1
  151.9 19.3 %copy-start = (f32[384,512]{1,0:T(8,128)S(1)}, f32[384,512]{1,0:T(8,128)}, u32[]{:S(2)}) copy-start(f32[384,512]{1,0:T(8,128)} %param.16) | copy-start | bytes 2359300
  151.9 19.3 %copy-start.3 = (f32[384,512]{1,0:T(8,128)S(1)}, f32[384,512]{1,0:T(8,128)}, u32[]{:S(2)}) copy-start(f32[384,512]{1,0:T(8,128)} %param.17) | copy-start | bytes 2359300
Sparse Core Ops, SparseCore 0:
  9.8 30.9 all-gather.9
  42.6 29.1 all-gather.11
  80.3 27.9 reduce-scatter.2
  110.5 29.1 all-gather.7
  142.0 27.4 all-gather.13
  172.4 99.5 reduce-scatter.4
